TPU v7x, 32 devices: a whole 2x2x4 slice. The times are simulated.
32 devices in a mesh: groups: 2 (over y), ctx: 4 (over z), mp: 4 (over x, core).
Axes of the slice: x: 2, y: 2, z: 4, core: 2. Of those that a mesh axis runs over, the one named last changes fastest.
Arguments:
- features: bfloat16 [4, 512, 1536], P('groups', 'ctx'), parts along dimension 0, may hold values from -6 to 6
- frame_counts: int32 [4], P('groups'), parts along dimension 0, may hold values from 1 to 512, 768 in all
- attn_gain: float32 [1536], replicated, may hold values from 0.25 to 1.75
- w_qkv: bfloat16 [3, 1536, 1024], P(None, None, 'mp'), may hold values from -2 to 2
- w_out: bfloat16 [1024, 1536], P('mp'), may hold values from -0.375 to 0.375
- conv_gain: float32 [1536], replicated, may hold values from 0.25 to 1.75
- w_glu: bfloat16 [2, 1536, 1536], P(None, None, 'mp'), may hold values from -0.15625 to 0.15625
- kernel: float32 [31, 1536], P(None, 'mp'), may hold values from -2 to 2
- bn_scale: float32 [1536], P('mp'), may hold values from 0.5 to 2
- bn_shift: float32 [1536], P('mp'), may hold values from -2.5 to 2.5
- w_pw: bfloat16 [1536, 1536], P('mp'), may hold values from -0.15625 to 0.15625
- clip_level: int32 [1536], replicated, may hold values from 6 to 39
Outputs:
- encoded: bfloat16 [4, 512, 1536], P('groups', ('ctx', 'mp')), parts along dimension 0
There are 2 independent parts, one for each index of `groups`. A program takes and returns all parts, laid end to end along the dimension named above; an argument that names none is the same for every part. Nothing has to cross between parts.
Inputs may be any that keep to these rules, and one draw needn't show every extreme that they name: frame_counts[s] frames of recording s fill slots 0 to frame_counts[s] - 1, later slots are padding; some recording fills all 512 slots.
All inputs are finite; a program needn't handle non-finite values.
Results may differ from a plain program's by a relative error of at most 0.023.
Values may be sent and summed in bfloat16 or wider, within the bound.
No kernel may reach another device: no remote copies, remote signals or barrier semaphores. Data moves between devices by JAX's collectives and lax.ppermute only.
A program may use at most 128 MiB of HBM per device.

v0:
```python
import jax
import jax.numpy as jnp
from jax import lax
from jax.sharding import PartitionSpec as P

HEAD_DIM = 64
epsilon = 1e-05
masked_score = -1e30


def with_halo(x, sides, width):
    for axis, dim in sides:
        devices, length = (lax.axis_size(axis), x.shape[dim])
        up = [(i, (i + 1) % devices) for i in range(devices - 1)]
        down = [(j, i) for i, j in up]
        last = lax.slice_in_dim(x, length - width, length, axis=dim)
        initial = lax.slice_in_dim(x, 0, width, axis=dim)
        before = lax.ppermute(last, axis, up)
        after = lax.ppermute(initial, axis, down)
        x = jnp.concatenate([before, x, after], axis=dim)
    return x


def layer_norm(values, gain):
    centre = jnp.mean(values, axis=-1, keepdims=True)
    centred = values - centre
    variance = jnp.mean(centred * centred, axis=-1, keepdims=True)
    return centred * lax.rsqrt(variance + epsilon) * gain


def gated_units(normed, w_glu):
    halves = jnp.einsum("std,gdc->gstc", normed, w_glu, preferred_element_type=jnp.float32)
    return (halves[0] * jax.nn.sigmoid(halves[1])).astype(jnp.bfloat16)


def shards(
    features,
    frame_counts,
    attn_gain,
    w_qkv,
    w_out,
    conv_gain,
    w_glu,
    kernel,
    bn_scale,
    bn_shift,
    w_pw,
    clip_level,
):
    records, frames_here, model_width = features.shape
    head_count = w_qkv.shape[2] // HEAD_DIM
    ctx_rank = lax.axis_index("ctx")
    score_scale = HEAD_DIM ** (-0.5)
    first_frame = ctx_rank * frames_here
    normed = layer_norm(features.astype(jnp.float32), attn_gain).astype(jnp.bfloat16)
    projected = jnp.einsum(
        "std,idc->istc", normed, w_qkv, preferred_element_type=jnp.float32
    ).astype(jnp.bfloat16)
    queries, key_rows, value_rows = (projected[0], projected[1], projected[2])
    query_heads = queries.reshape(records, frames_here, head_count, HEAD_DIM)
    start_max = jnp.full((records, head_count, frames_here), masked_score, jnp.float32)
    pieces = (
        lax.all_gather(key_rows, "ctx", axis=1, tiled=True),
        lax.all_gather(value_rows, "ctx", axis=1, tiled=True),
    )
    key_count = pieces[0].shape[1]
    key_heads = pieces[0].reshape(records, key_count, head_count, HEAD_DIM)
    value_heads = pieces[1].reshape(records, key_count, head_count, HEAD_DIM)
    scores = (
        jnp.einsum("sqhe,skhe->shqk", query_heads, key_heads, preferred_element_type=jnp.float32)
        * score_scale
    )
    positions = jnp.arange(key_count, dtype=jnp.int32)
    is_live = positions[None, :] < frame_counts[:, None]
    scores = jnp.where(is_live[:, None, None, :], scores, masked_score)
    new_max = jnp.maximum(start_max, jnp.max(scores, axis=-1))
    weights = jnp.exp(scores - new_max[..., None])
    new_sum = jnp.sum(weights, axis=-1)
    contrib = jnp.einsum(
        "shqk,skhe->shqe",
        weights.astype(jnp.bfloat16),
        value_heads,
        preferred_element_type=jnp.float32,
    )
    attended = (contrib / new_sum[..., None]).astype(jnp.bfloat16)
    attended = attended.transpose(0, 2, 1, 3).reshape(records, frames_here, head_count * HEAD_DIM)
    attn_part = jnp.einsum("stc,cd->std", attended, w_out, preferred_element_type=jnp.float32)
    mp_count = lax.axis_size("mp")
    mp_rank = lax.axis_index("mp")
    rows_mine = frames_here // mp_count
    row_start = mp_rank * rows_mine
    attn_sum = lax.psum(attn_part.astype(jnp.bfloat16), "mp").astype(jnp.float32)
    residual = features.astype(jnp.float32) + attn_sum
    gated_rows = gated_units(layer_norm(residual, conv_gain).astype(jnp.bfloat16), w_glu)
    residual_mine = lax.dynamic_slice_in_dim(residual, row_start, rows_mine, 1)
    frame_ids = first_frame + jnp.arange(frames_here, dtype=jnp.int32)
    frame_live = frame_ids[None, :] < frame_counts[:, None]
    gated_rows = jnp.where(frame_live[..., None], gated_rows, jnp.zeros((), jnp.bfloat16))
    rim_width = kernel.shape[0] // 2
    padded = with_halo(gated_rows, (("ctx", 1),), rim_width)
    depthwise = jnp.zeros(gated_rows.shape, jnp.float32)
    for tap_index in range(kernel.shape[0]):
        depthwise = (
            depthwise
            + padded[:, tap_index : tap_index + frames_here, :].astype(jnp.float32)
            * kernel[tap_index]
        )
    activated = jax.nn.silu(depthwise * bn_scale + bn_shift).astype(jnp.bfloat16)
    conv_part = jnp.einsum("stc,cd->std", activated, w_pw, preferred_element_type=jnp.float32)
    conv_rows = lax.psum_scatter(
        conv_part.astype(jnp.bfloat16), "mp", scatter_dimension=1, tiled=True
    ).astype(jnp.float32)
    combined = residual_mine + conv_rows
    clip_bound = clip_level.astype(jnp.float32) / 16.0
    clipped = jnp.clip(combined, -clip_bound, clip_bound)
    mine_ids = first_frame + row_start + jnp.arange(rows_mine, dtype=jnp.int32)
    mine_live = mine_ids[None, :] < frame_counts[:, None]
    return jnp.where(mine_live[..., None], clipped, 0.0).astype(jnp.bfloat16)


def solution(mesh):
    return jax.shard_map(
        shards,
        mesh=mesh,
        in_specs=(
            P("groups", "ctx", None),
            P("groups"),
            P(),
            P(None, None, "mp"),
            P("mp", None),
            P(),
            P(None, None, "mp"),
            P(None, "mp"),
            P("mp"),
            P("mp"),
            P("mp", None),
            P(),
        ),
        out_specs=P("groups", ("ctx", "mp"), None),
        check_vma=False,
    )
```

profile of v0, /device:TPU:0, one launch (start us, length us, event | category | flops | bytes accessed | tf_op | source)
XLA Modules:
  0.0 141.7 jit_solution(3153262464073058169)
XLA Ops:
  6.5 0.0 copy-start
  6.5 0.0 all-reduce.2.cloned.1.call-start
  6.5 1.5 %convert_reduce_fusion = f32[2,128]{1,0:T(2,128)S(1)} fusion(bf16[2,128,1536]{2,1,0:T(8,128)(2,1)} %param.12), kind=kLoop, calls=%fused_computation.4 | loop fusion | flops 786176 | bytes 787456 | tf_op jit(solution)/shard_map/reduce_sum | solution.py:25
  8.0 1.5 %fusion.9 = f32[2,128]{1,0:T(2,128)S(1)} fusion(bf16[2,128,1536]{2,1,0:T(8,128)(2,1)} %param.12, f32[2,128]{1,0:T(2,128)S(1)} %broadcast_multiply_fusion.1), kind=kLoop, calls=%fused_computation.16 | loop fusion | flops 1572608 | bytes 788480 | tf_op jit(solution)/shard_map/reduce_sum | solution.py:27
  9.5 0.0 copy-done
  9.5 0.0 copy-done.1
  9.5 0.0 copy-done.10
  9.5 0.8 fusion.18
  10.4 0.0 copy-start.7
  10.5 18.0 %all-gather = bf16[1,2,512,256]{3,2,0,1:T(8,128)(2,1)} all-gather(bf16[1,2,128,256]{3,2,0,1:T(8,128)(2,1)S(1)} %get-tuple-element.38), channel_id=2, replica_groups=mesh['groups'=2,'ctx'=4,'mp'=4] {'ctx'}, dimensions={2}, use_global_device_ids=true | all-gather | bytes 655360 | tf_op jit(solution)/shard_map/all_gather | solution.py:63
  28.5 2.0 %copy.18 = bf16[1,2,512,256]{2,3,1,0:T(8,128)(2,1)} copy(bf16[1,2,512,256]{3,2,0,1:T(8,128)(2,1)} %all-gather) | data formatting | bytes 1048576 | tf_op jit(solution)/shard_map/all_gather | solution.py:63
  30.5 0.1 copy.17
  30.6 0.0 copy-done.7
  30.6 0.1 iota_compare_fusion
  30.7 2.9 %fusion.6 = (f32[2,4,128]{2,1,0:T(4,128)S(1)}, f32[2,4,128,512]{3,2,1,0:T(8,128)}) fusion(pred[2,512]{1,0:T(4,128)(4,1)S(1)} %iota_compare_fusion, bf16[2,128,4,64]{1,3,2,0:T(8,128)(2,1)S(1)} %bitcast.50, bf16[2,512,4,64]{1,3,2,0:T(8,128)(2,1)} %bitcast.49), kind=kOutput, calls=%fused_computation.13 | convolution fusion | flops 68680704 | bytes 2757632 | tf_op jit(solution)/shard_map/sqhe,skhe->shqk/dot_general | solution.py:70
  33.6 17.0 %all-gather.1 = bf16[1,2,512,256]{3,2,0,1:T(8,128)(2,1)} all-gather(bf16[1,2,128,256]{3,2,0,1:T(8,128)(2,1)S(1)} %get-tuple-element.39), channel_id=3, replica_groups=mesh['groups'=2,'ctx'=4,'mp'=4] {'ctx'}, dimensions={2}, use_global_device_ids=true | all-gather | bytes 655360 | tf_op jit(solution)/shard_map/all_gather | solution.py:64
  50.6 2.1 %copy.19 = bf16[1,2,512,256]{2,3,1,0:T(8,128)(2,1)} copy(bf16[1,2,512,256]{3,2,0,1:T(8,128)(2,1)} %all-gather.1) | data formatting | bytes 1048576 | tf_op jit(solution)/shard_map/all_gather | solution.py:64
  52.6 2.3 %fusion.7 = f32[2,4,128]{2,1,0:T(4,128)S(1)} fusion(f32[2,4,128,512]{3,2,1,0:T(8,128)} %get-tuple-element.46, f32[2,4,128]{2,1,0:T(4,128)S(1)} %broadcast_maximum_fusion, pred[2,512]{1,0:T(4,128)(4,1)S(1)} %iota_compare_fusion), kind=kLoop, calls=%fused_computation.14 | loop fusion | flops 2096128 | bytes 2106368 | tf_op jit(solution)/shard_map/reduce_sum | solution.py:78
  54.9 0.0 copy-done.2
  55.0 0.0 copy-start.4
  55.0 1.8 %fusion.23 = bf16[2,128,4,64]{1,3,2,0:T(8,128)(2,1)S(1)} fusion(bf16[2,512,4,64]{1,3,2,0:T(8,128)(2,1)} %bitcast.51, f32[2,4,128,512]{3,2,1,0:T(8,128)S(1)} %copy-done.2, f32[2,4,128]{2,1,0:T(4,128)S(1)} %broadcast_maximum_fusion, pred[2,512]{1,0:T(4,128)(4,1)S(1)} %iota_compare_fusion, f32[2,128,4]{1,2,0:T(4,128)S(1)} %bitcast.53), kind=kOutput, calls=%fused_computation.55 | convolution fusion | flops 69337088 | bytes 2761728 | tf_op jit(solution)/shard_map/shqk,skhe->shqe/dot_general | solution.py:79
  56.8 0.0 copy-start.5
  56.8 0.0 copy-done.4
  56.8 1.3 convolution_convert_fusion
  58.1 0.0 all-reduce.2.cloned.1.call-update
  58.1 0.0 reduce-scatter.2.cloned.1.call-start
  58.2 0.0 copy-done.5
  58.2 0.1 slice_reduce_fusion.30
  58.3 0.1 broadcast_compare_fusion
  58.3 35.0 %all-reduce.2.cloned.1.call-done = bf16[2,128,1536]{2,1,0:T(8,128)(2,1)} async-done(((bf16[2,128,1536]{2,1,0:T(8,128)(2,1)}), bf16[2,128,1536]{2,1,0:T(8,128)(2,1)}) %all-reduce.2.cloned.1.call-update) | async-done | bytes 786448 | tf_op jit(solution)/shard_map/psum | solution.py:92
  93.3 2.6 %convert_add_fusion = (f32[2,128,1536]{2,1,0:T(8,128)}, f32[2,128]{1,0:T(2,128)S(1)}) fusion(bf16[2,128,1536]{2,1,0:T(8,128)(2,1)S(1)} %copy-done.1, bf16[2,128,1536]{2,1,0:T(8,128)(2,1)} %all-reduce.2.cloned.1.call-done), kind=kLoop, calls=%fused_computation.2 | loop fusion | flops 1572608 | bytes 3146752 | tf_op jit(solution)/shard_map/add | solution.py:93
  96.0 0.0 copy-done.3
  96.0 0.4 multiply_reduce_fusion
  96.4 0.0 copy-done.8
  96.4 0.3 copy-done.11
  96.7 1.0 fusion.12
  97.7 0.1 bitcast_select_fusion
  97.8 3.4 %collective-permute-start = (bf16[2,15,384]{2,1,0:T(8,128)(2,1)S(1)}, bf16[2,15,384]{2,1,0:T(8,128)(2,1)S(1)}, u32[]{:S(2)}, u32[]{:S(2)}) collective-permute-start(bf16[2,15,384]{2,1,0:T(8,128)(2,1)S(1)} %get-tuple-element.41), channel_id=1, source_target_pairs={{0,4},{4,8},{8,12},{1,5},{5,9},{9,13},{2,6},{6,10},{10,14},{3,7},{... | collective-permute-start | bytes 69128 | tf_op jit(solution)/shard_map/ppermute | solution.py:18
  101.2 1.3 collective-permute-start.1
  102.5 0.1 slice_reduce_fusion.29
  102.6 0.1 collective-permute-done
  102.7 4.2 %collective-permute-done.1 = bf16[2,15,384]{2,1,0:T(8,128)(2,1)S(1)} collective-permute-done((bf16[2,15,384]{2,1,0:T(8,128)(2,1)S(1)}, bf16[2,15,384]{2,1,0:T(8,128)(2,1)S(1)}, u32[]{:S(2)}, u32[]{:S(2)}) %collective-permute-start.1) | collective-permute-done | bytes 23072 | tf_op jit(solution)/shard_map/ppermute | solution.py:19
  106.9 0.0 copy-start.6
  107.0 3.5 %convolution_convert_fusion.1 = bf16[2,128,1536]{2,1,0:T(8,128)(2,1)} fusion(bf16[384,1536]{1,0:T(8,128)(2,1)S(1)} %copy-done.9, bf16[2,128,384]{2,1,0:T(8,128)(2,1)S(1)} %bitcast_select_fusion, bf16[2,15,384]{2,1,0:T(8,128)(2,1)S(1)} %collective-permute-done.1, bf16[2,15,384]{2,1,0:T(8,128)(2,1)S(1)} %collective-permute-done, f32[384]{0:T(512)S(1)} %copy-done.12, ...), kind=kOutput, calls=%fused_computation.1 | convolution fusion | flops 320962560 | bytes 2259456 | tf_op jit(solution)/shard_map/stc,cd->std/dot_general | solution.py:109
  110.5 0.0 reduce-scatter.2.cloned.1.call-update
  110.5 0.1 broadcast_compare_fusion.1
  110.6 22.4 %reduce-scatter.2.cloned.1.call-done = bf16[2,32,1536]{2,1,0:T(8,128)(2,1)} async-done(((bf16[2,128,1536]{2,1,0:T(8,128)(2,1)}), bf16[2,32,1536]{2,1,0:T(8,128)(2,1)}) %reduce-scatter.2.cloned.1.call-update) | async-done | bytes 196624 | tf_op jit(solution)/shard_map/reduce_scatter | solution.py:110
  133.0 1.9 %select_convert_fusion = bf16[2,32,1536]{2,1,0:T(8,128)(2,1)} fusion(bf16[2,32,1536]{2,1,0:T(8,128)(2,1)} %reduce-scatter.2.cloned.1.call-done, f32[2,128,1536]{2,1,0:T(8,128)} %get-tuple-element.36, s32[]{:T(128)S(6)} %select_n.16, bf16[1536]{0:T(1024)(128)(2,1)S(1)} %get-tuple-element.44, bf16[1536]{0:T(1024)(128)(2,1)S(1)} %get-tuple-element.43, ...), kind=kLoop, calls=%fused_computation.74 | loop fusion | flops 786432 | bytes 792644 | tf_op jit(solution)/shard_map/convert_element_type | solution.py:118
  (23 shorter events, 0.1 us)
Async XLA Ops:
  6.5 3.0 %copy-start = (bf16[3,1536,256]{2,1,0:T(8,128)(2,1)S(1)}, bf16[3,1536,256]{2,1,0:T(8,128)(2,1)}, u32[]{:S(2)}) copy-start(bf16[3,1536,256]{2,1,0:T(8,128)(2,1)} %param.15) | copy-start | bytes 7077892
  6.5 3.0 %copy-start.1 = (bf16[2,128,1536]{2,1,0:T(8,128)(2,1)S(1)}, bf16[2,128,1536]{2,1,0:T(8,128)(2,1)}, u32[]{:S(2)}) copy-start(bf16[2,128,1536]{2,1,0:T(8,128)(2,1)} %param.12) | copy-start | bytes 2359300
  6.5 3.0 %copy-start.10 = (f32[1536]{0:T(1024)S(1)}, f32[1536]{0:T(1024)}, u32[]{:S(2)}) copy-start(f32[1536]{0:T(1024)} %param.14) | copy-start | bytes 18436
  6.5 86.8 %all-reduce.2.cloned.1.call-start = ((), (), s32[]{:S(2)}) async-start(), calls=%async_computation.1 | async-start | bytes 1572864 | tf_op jit(solution)/shard_map/psum | solution.py:92
  10.4 20.2 %copy-start.7 = (s32[2]{0:T(128)S(1)}, s32[2]{0:T(128)}, u32[]{:S(2)}) copy-start(s32[2]{0:T(128)} %param.13) | copy-start | bytes 28
  52.6 2.3 %copy-start.2 = (f32[2,4,128,512]{3,2,1,0:T(8,128)S(1)}, f32[2,4,128,512]{3,2,1,0:T(8,128)}, u32[]{:S(2)}) copy-start(f32[2,4,128,512]{3,2,1,0:T(8,128)} %get-tuple-element.46) | copy-start | bytes 6291460
  55.0 1.8 %copy-start.4 = (bf16[256,1536]{1,0:T(8,128)(2,1)S(1)}, bf16[256,1536]{1,0:T(8,128)(2,1)}, u32[]{:S(2)}) copy-start(bf16[256,1536]{1,0:T(8,128)(2,1)} %param.16) | copy-start | bytes 2359300
  56.8 1.4 copy-start.5
  58.1 74.9 %reduce-scatter.2.cloned.1.call-start = ((), (), s32[]{:S(2)}) async-start(), calls=%async_computation.2 | async-start | bytes 983040 | tf_op jit(solution)/shard_map/reduce_scatter | solution.py:110
  93.3 2.7 %copy-start.3 = (bf16[2,128,1536]{2,1,0:T(8,128)(2,1)S(1)}, bf16[2,128,1536]{2,1,0:T(8,128)(2,1)}, u32[]{:S(2)}) copy-start(bf16[2,128,1536]{2,1,0:T(8,128)(2,1)} %all-reduce.2.cloned.1.call-done) | copy-start | bytes 2359300
  93.3 3.1 %copy-start.8 = (bf16[2,1536,384]{2,1,0:T(8,128)(2,1)S(1)}, bf16[2,1536,384]{2,1,0:T(8,128)(2,1)}, u32[]{:S(2)}) copy-start(bf16[2,1536,384]{2,1,0:T(8,128)(2,1)} %param.18) | copy-start | bytes 7077892
  96.0 0.7 copy-start.11
  96.7 10.2 %copy-start.9 = (bf16[384,1536]{1,0:T(8,128)(2,1)S(1)}, bf16[384,1536]{1,0:T(8,128)(2,1)}, u32[]{:S(2)}) copy-start(bf16[384,1536]{1,0:T(8,128)(2,1)} %param.22) | copy-start | bytes 3538948
  96.7 10.2 %copy-start.12 = (f32[384]{0:T(512)S(1)}, f32[384]{0:T(512)}, u32[]{:S(2)}) copy-start(f32[384]{0:T(512)} %param.21) | copy-start | bytes 4612
  96.7 10.2 %copy-start.13 = (f32[384]{0:T(512)S(1)}, f32[384]{0:T(512)}, u32[]{:S(2)}) copy-start(f32[384]{0:T(512)} %param.20) | copy-start | bytes 4612
  97.8 4.9 %collective-permute-start = (bf16[2,15,384]{2,1,0:T(8,128)(2,1)S(1)}, bf16[2,15,384]{2,1,0:T(8,128)(2,1)S(1)}, u32[]{:S(2)}, u32[]{:S(2)}) collective-permute-start(bf16[2,15,384]{2,1,0:T(8,128)(2,1)S(1)} %get-tuple-element.41), channel_id=1, source_target_pairs={{0,4},{4,8},{8,12},{1,5},{5,9},{9,13},{2,6},{6,10},{10,14},{3,7},{... | collective-permute-start | bytes 69128 | tf_op jit(solution)/shard_map/ppermute | solution.py:18
  101.2 5.7 %collective-permute-start.1 = (bf16[2,15,384]{2,1,0:T(8,128)(2,1)S(1)}, bf16[2,15,384]{2,1,0:T(8,128)(2,1)S(1)}, u32[]{:S(2)}, u32[]{:S(2)}) collective-permute-start(bf16[2,15,384]{2,1,0:T(8,128)(2,1)S(1)} %get-tuple-element.42), channel_id=1, source_target_pairs={{4,0},{8,4},{12,8},{5,1},{9,5},{13,9},{6,2},{10,6},{14,10},{7,3},{... | collective-permute-start | bytes 69128 | tf_op jit(solution)/shard_map/ppermute | solution.py:19
  106.9 3.7 %copy-start.6 = (s32[1536]{0:T(1024)S(1)}, s32[1536]{0:T(1024)}, u32[]{:S(2)}) copy-start(s32[1536]{0:T(1024)} %param.23) | copy-start | bytes 18436
Sparse Core Ops, SparseCore 0:
  58.2 35.0 all-reduce.1
  110.6 22.3 reduce-scatter.1
where the time goes:
time: 142 us
  waiting for transfers between devices  61.8 us (44%)
  blocking collectives  35 us (25%)
  between operations  13.6 us (10%)
  matrix products  11.3 us (8%)
  other arithmetic  10.6 us (7%)
  local copies, waits for them, and re-layouts  4.75 us (3%)
  starting transfers between devices  4.72 us (3%)
    psum x1, waiting for transfers between devices, shards(): lax.psum(attn_part.astype(jnp.bfloat16), 'mp').astype(jnp.float32)  35 us
    reduce_scatter x1, waiting for transfers between devices, shards(): lax.psum_scatter(conv_part.astype(jnp.bfloat16), 'mp', scatter_dimension=...  22.4 us
    all_gather x1, blocking collectives, shards(): lax.all_gather(key_rows, 'ctx', axis=1, tiled=True)  18 us
    all_gather x1, blocking collectives, shards(): lax.all_gather(value_rows, 'ctx', axis=1, tiled=True)  17 us
    ppermute x1, waiting for transfers between devices, with_halo(): after = lax.ppermute(initial, axis, down)  4.22 us
    dot_general x1, matrix products, shards(): jnp.einsum('stc,cd->std', activated, w_pw, preferred_element_type=jnp.flo...  3.55 us
    ppermute x1, starting transfers between devices, with_halo(): before = lax.ppermute(last, axis, up)  3.39 us
    dot_general x1, matrix products, shards(): jnp.einsum('sqhe,skhe->shqk', query_heads, key_heads, preferred_element_t...  2.88 us
  transfers between devices with their start and end apart: 4, of which 4 were waited for; matrix products, arithmetic and copies ran while one was open for 0% of the time, Pallas kernels for 0%

commit v1 on v0

--- a/solution.py
+++ b/solution.py
@@ -6,6 +6,27 @@
 HEAD_DIM = 64
 epsilon = 1e-05
 masked_score = -1e30
+
+
+def ring_gather(x, axis, dim):
+    count, index, rows = (lax.axis_size(axis), lax.axis_index(axis), x.shape[dim])
+    ahead = [(i, (i + 1) % count) for i in range(count)]
+    left = [(i, (i - 1) % count) for i in range(count)]
+    whole = jnp.zeros((*x.shape[:dim], count * rows, *x.shape[dim + 1 :]), x.dtype)
+    whole = lax.dynamic_update_slice_in_dim(whole, x, index * rows, axis=dim)
+    from_left = from_right = x
+    half = count // 2
+    for lap in range(1, half + 1):
+        from_left = lax.ppermute(from_left, axis, ahead)
+        whole = lax.dynamic_update_slice_in_dim(
+            whole, from_left, (index - lap) % count * rows, axis=dim
+        )
+        if lap < count - half:
+            from_right = lax.ppermute(from_right, axis, left)
+            whole = lax.dynamic_update_slice_in_dim(
+                whole, from_right, (index + lap) % count * rows, axis=dim
+            )
+    return whole
 
 
 def with_halo(x, sides, width):
@@ -61,7 +82,7 @@
     start_max = jnp.full((records, head_count, frames_here), masked_score, jnp.float32)
     pieces = (
         lax.all_gather(key_rows, "ctx", axis=1, tiled=True),
-        lax.all_gather(value_rows, "ctx", axis=1, tiled=True),
+        ring_gather(value_rows, "ctx", 1),
     )
     key_count = pieces[0].shape[1]
     key_heads = pieces[0].reshape(records, key_count, head_count, HEAD_DIM)

time: 142 us -> 136 us (0.958)
  blocking collectives: 35 us -> 17.8 us
  starting transfers between devices: 4.72 us -> 10.2 us
  local copies, waits for them, and re-layouts: 4.75 us -> 9.88 us
  waiting for transfers between devices: 61.8 us -> 64.2 us
  other arithmetic: 10.6 us -> 8.87 us
    all_gather x1 -> x0, blocking collectives: 17 us -> none  [shards(): lax.all_gather(value_rows, 'ctx', axis=1, tiled=True)]
    ppermute x0 -> x3, starting transfers between devices: none -> 5.49 us  [the longest x2 3.39 us: ring_gather(): from_left = lax.ppermute(from_left, axis, ahead)]
    ppermute x0 -> x3, waiting for transfers between devices: none -> 4.32 us  [the longest x2 4.31 us: ring_gather(): from_left = lax.ppermute(from_left, axis, ahead)]
    dynamic_update_slice x0 -> x4, local copies, waits for them, and re-layouts: none -> 2.71 us  [the longest x2 1.37 us: ring_gather(): lax.dynamic_update_slice_in_dim(whole, from_left, (index - lap) % count *...]
    ppermute x0 -> x3, local copies, waits for them, and re-layouts: none -> 2.16 us  [the longest x2 1.14 us: ring_gather(): from_left = lax.ppermute(from_left, axis, ahead)]
    all_gather x1 -> x0, local copies, waits for them, and re-layouts: 2.05 us -> none  [shards(): lax.all_gather(value_rows, 'ctx', axis=1, tiled=True)]
    psum x1, waiting for transfers between devices: 35 us -> 33 us  [shards(): lax.psum(attn_part.astype(jnp.bfloat16), 'mp').astype(jnp.float32)]
    reduce_sum x1, other arithmetic: 2.3 us -> 0.61 us  [shards(): new_sum = jnp.sum(weights, axis=-1)]
  transfers between devices with their start and end apart: 4 -> 7, of which waited for: 4 -> 5; matrix products, arithmetic and copies ran while one was open for 0% -> 7% of each run, Pallas kernels for 0% -> 0%
where the time goes in v1:
time: 136 us; the launch traced here: 135 us
  waiting for transfers between devices  64.2 us (47%)
  blocking collectives  17.8 us (13%)
  between operations  13.7 us (10%)
  matrix products  10.6 us (8%)
  starting transfers between devices  10.2 us (7%)
  local copies, waits for them, and re-layouts  9.88 us (7%)
  other arithmetic  8.87 us (7%)
    psum x1, waiting for transfers between devices, shards(): lax.psum(attn_part.astype(jnp.bfloat16), 'mp').astype(jnp.float32)  33 us
    reduce_scatter x1, waiting for transfers between devices, shards(): lax.psum_scatter(conv_part.astype(jnp.bfloat16), 'mp', scatter_dimension=...  22.5 us
    all_gather x1, blocking collectives, shards(): lax.all_gather(key_rows, 'ctx', axis=1, tiled=True)  17.8 us
    ppermute x2, waiting for transfers between devices, ring_gather(): from_left = lax.ppermute(from_left, axis, ahead)  4.31 us
    ppermute x1, waiting for transfers between devices, with_halo(): after = lax.ppermute(initial, axis, down)  4.22 us
    dot_general x1, matrix products, shards(): jnp.einsum('stc,cd->std', activated, w_pw, preferred_element_type=jnp.flo...  3.52 us
    ppermute x2, starting transfers between devices, ring_gather(): from_left = lax.ppermute(from_left, axis, ahead)  3.39 us
    ppermute x1, starting transfers between devices, with_halo(): before = lax.ppermute(last, axis, up)  3.39 us
  transfers between devices with their start and end apart: 7, of which 5 were waited for; matrix products, arithmetic and copies ran while one was open for 7% of the time, Pallas kernels for 0%

profile of v1, /device:TPU:0, one launch (start us, length us, event | category | flops | bytes accessed | tf_op | source)
XLA Modules:
  0.0 135.2 jit_solution(325660195085175890)
XLA Ops:
  6.5 1.5 %convert_reduce_fusion = f32[2,128]{1,0:T(2,128)S(1)} fusion(bf16[2,128,1536]{2,1,0:T(8,128)(2,1)} %param.12), kind=kLoop, calls=%fused_computation.4 | loop fusion | flops 786176 | bytes 787456 | tf_op jit(solution)/shard_map/reduce_sum | solution.py:46
  8.0 1.5 %fusion.9 = f32[2,128]{1,0:T(2,128)S(1)} fusion(bf16[2,128,1536]{2,1,0:T(8,128)(2,1)} %param.12, f32[2,128]{1,0:T(2,128)S(1)} %broadcast_multiply_fusion.1), kind=kLoop, calls=%fused_computation.16 | loop fusion | flops 1572608 | bytes 788480 | tf_op jit(solution)/shard_map/reduce_sum | solution.py:48
  9.5 0.8 fusion.18
  10.4 0.0 copy-start.7
  10.5 3.1 %collective-permute-start = (bf16[2,128,256]{2,1,0:T(8,128)(2,1)S(1)}, bf16[2,128,256]{2,1,0:T(8,128)(2,1)}, u32[]{:S(2)}, u32[]{:S(2)}) collective-permute-start(bf16[2,128,256]{2,1,0:T(8,128)(2,1)S(1)} %get-tuple-element.39), channel_id=1, source_target_pairs={{0,4},{4,8},{8,12},{12,0},{1,5},{5,9},{9,13},{13,1},{2,6},{6,10},{... | collective-permute-start | bytes 393224 | tf_op jit(solution)/shard_map/ppermute | solution.py:20
  13.5 2.1 %collective-permute-start.1 = (bf16[2,128,256]{2,1,0:T(8,128)(2,1)S(1)}, bf16[2,128,256]{2,1,0:T(8,128)(2,1)}, u32[]{:S(2)}, u32[]{:S(2)}) collective-permute-start(bf16[2,128,256]{2,1,0:T(8,128)(2,1)S(1)} %get-tuple-element.39), channel_id=1, source_target_pairs={{0,12},{4,0},{8,4},{12,8},{1,13},{5,1},{9,5},{13,9},{2,14},{6,2},{... | collective-permute-start | bytes 393224 | tf_op jit(solution)/shard_map/ppermute | solution.py:25
  15.6 17.8 %all-gather = bf16[1,2,512,256]{3,2,0,1:T(8,128)(2,1)} all-gather(bf16[1,2,128,256]{3,2,0,1:T(8,128)(2,1)S(1)} %get-tuple-element.38), channel_id=2, replica_groups=mesh['groups'=2,'ctx'=4,'mp'=4] {'ctx'}, dimensions={2}, use_global_device_ids=true | all-gather | bytes 655360 | tf_op jit(solution)/shard_map/all_gather | solution.py:84
  33.4 2.1 %copy.21 = bf16[1,2,512,256]{2,3,1,0:T(8,128)(2,1)} copy(bf16[1,2,512,256]{3,2,0,1:T(8,128)(2,1)} %all-gather) | data formatting | bytes 1048576 | tf_op jit(solution)/shard_map/all_gather | solution.py:84
  35.5 0.1 copy.20
  35.6 0.1 iota_compare_fusion
  35.7 1.6 %fusion.6 = (f32[2,4,128]{2,1,0:T(4,128)S(1)}, f32[2,4,128,512]{3,2,1,0:T(8,128)S(1)}) fusion(pred[2,512]{1,0:T(4,128)(4,1)S(1)} %iota_compare_fusion, bf16[2,128,4,64]{1,3,2,0:T(8,128)(2,1)S(1)} %bitcast.52, bf16[2,512,4,64]{1,3,2,0:T(8,128)(2,1)} %bitcast.51), kind=kOutput, calls=%fused_computation.13 | convolution fusion | flops 68680704 | bytes 2757632 | tf_op jit(solution)/shard_map/sqhe,skhe->shqk/dot_general | solution.py:91
  37.3 1.3 copy-done.2
  38.6 0.6 fusion.7
  39.2 0.1 copy.22
  39.4 0.8 broadcast_in_dim.44
  40.2 0.7 constant_dynamic-update-slice_fusion.3
  40.9 1.0 copy.23
  41.9 0.3 collective-permute-start.2
  42.2 0.7 constant_dynamic-update-slice_fusion.2
  42.9 1.0 copy.24
  43.9 0.7 constant_dynamic-update-slice_fusion.1
  44.6 4.3 %collective-permute-done.2 = bf16[2,128,256]{2,1,0:T(8,128)(2,1)S(1)} collective-permute-done((bf16[2,128,256]{2,1,0:T(8,128)(2,1)}, bf16[2,128,256]{2,1,0:T(8,128)(2,1)S(1)}, u32[]{:S(2)}, u32[]{:S(2)}) %collective-permute-start.2) | collective-permute-done | bytes 131104 | tf_op jit(solution)/shard_map/ppermute | solution.py:20
  48.9 0.1 copy.25
  49.1 0.7 constant_dynamic-update-slice_fusion
  49.7 2.4 %fusion.23 = bf16[2,128,4,64]{1,3,2,0:T(8,128)(2,1)S(1)} fusion(bf16[2,512,4,64]{1,3,2,0:T(8,128)(2,1)} %bitcast.7, f32[2,4,128,512]{3,2,1,0:T(8,128)} %copy-done.2, f32[2,4,128]{2,1,0:T(4,128)S(1)} %broadcast_maximum_fusion, pred[2,512]{1,0:T(4,128)(4,1)S(1)} %iota_compare_fusion, f32[2,128,4]{1,2,0:T(4,128)S(1)} %bitcast.54), kind=kOutput, calls=%fused_computation.55 | convolution fusion | flops 69337088 | bytes 2761728 | tf_op jit(solution)/shard_map/shqk,skhe->shqe/dot_general | solution.py:100
  52.2 0.0 copy-start.5
  52.2 1.3 convolution_convert_fusion
  53.5 0.0 all-reduce.2.cloned.1.call-update
  53.5 0.0 reduce-scatter.2.cloned.1.call-start
  53.5 0.1 slice_reduce_fusion.30
  53.7 0.1 broadcast_compare_fusion
  53.7 33.0 %all-reduce.2.cloned.1.call-done = bf16[2,128,1536]{2,1,0:T(8,128)(2,1)} async-done(((bf16[2,128,1536]{2,1,0:T(8,128)(2,1)}), bf16[2,128,1536]{2,1,0:T(8,128)(2,1)}) %all-reduce.2.cloned.1.call-update) | async-done | bytes 786448 | tf_op jit(solution)/shard_map/psum | solution.py:113
  86.8 2.6 %convert_add_fusion = (f32[2,128,1536]{2,1,0:T(8,128)}, f32[2,128]{1,0:T(2,128)S(1)}) fusion(bf16[2,128,1536]{2,1,0:T(8,128)(2,1)S(1)} %copy-done.1, bf16[2,128,1536]{2,1,0:T(8,128)(2,1)} %all-reduce.2.cloned.1.call-done), kind=kLoop, calls=%fused_computation.2 | loop fusion | flops 1572608 | bytes 3146752 | tf_op jit(solution)/shard_map/add | solution.py:114
  89.4 0.4 multiply_reduce_fusion
  89.8 0.3 copy-done.11
  90.1 1.0 fusion.12
  91.1 0.1 bitcast_select_fusion
  91.2 3.4 %collective-permute-start.3 = (bf16[2,15,384]{2,1,0:T(8,128)(2,1)S(1)}, bf16[2,15,384]{2,1,0:T(8,128)(2,1)S(1)}, u32[]{:S(2)}, u32[]{:S(2)}) collective-permute-start(bf16[2,15,384]{2,1,0:T(8,128)(2,1)S(1)} %get-tuple-element.41), channel_id=1, source_target_pairs={{0,4},{4,8},{8,12},{1,5},{5,9},{9,13},{2,6},{6,10},{10,14},{3,7},{... | collective-permute-start | bytes 69128 | tf_op jit(solution)/shard_map/ppermute | solution.py:39
  94.6 1.3 collective-permute-start.4
  95.9 0.1 slice_reduce_fusion.29
  96.0 0.1 collective-permute-done.3
  96.1 4.2 %collective-permute-done.4 = bf16[2,15,384]{2,1,0:T(8,128)(2,1)S(1)} collective-permute-done((bf16[2,15,384]{2,1,0:T(8,128)(2,1)S(1)}, bf16[2,15,384]{2,1,0:T(8,128)(2,1)S(1)}, u32[]{:S(2)}, u32[]{:S(2)}) %collective-permute-start.4) | collective-permute-done | bytes 23072 | tf_op jit(solution)/shard_map/ppermute | solution.py:40
  100.4 0.0 copy-start.6
  100.4 3.5 %convolution_convert_fusion.1 = bf16[2,128,1536]{2,1,0:T(8,128)(2,1)} fusion(bf16[384,1536]{1,0:T(8,128)(2,1)S(1)} %copy-done.9, bf16[2,128,384]{2,1,0:T(8,128)(2,1)S(1)} %bitcast_select_fusion, bf16[2,15,384]{2,1,0:T(8,128)(2,1)S(1)} %collective-permute-done.4, bf16[2,15,384]{2,1,0:T(8,128)(2,1)S(1)} %collective-permute-done.3, f32[384]{0:T(512)S(1)} %copy-done.12, ...), kind=kOutput, calls=%fused_computation.1 | convolution fusion | flops 320962560 | bytes 2259456 | tf_op jit(solution)/shard_map/stc,cd->std/dot_general | solution.py:130
  103.9 0.0 reduce-scatter.2.cloned.1.call-update
  103.9 0.1 broadcast_compare_fusion.1
  104.0 22.5 %reduce-scatter.2.cloned.1.call-done = bf16[2,32,1536]{2,1,0:T(8,128)(2,1)} async-done(((bf16[2,128,1536]{2,1,0:T(8,128)(2,1)}), bf16[2,32,1536]{2,1,0:T(8,128)(2,1)}) %reduce-scatter.2.cloned.1.call-update) | async-done | bytes 196624 | tf_op jit(solution)/shard_map/reduce_scatter | solution.py:131
  126.5 1.9 %select_convert_fusion = bf16[2,32,1536]{2,1,0:T(8,128)(2,1)} fusion(bf16[2,32,1536]{2,1,0:T(8,128)(2,1)} %reduce-scatter.2.cloned.1.call-done, f32[2,128,1536]{2,1,0:T(8,128)} %get-tuple-element.36, s32[]{:T(128)S(6)} %select_n.50, bf16[1536]{0:T(1024)(128)(2,1)S(1)} %get-tuple-element.44, bf16[1536]{0:T(1024)(128)(2,1)S(1)} %get-tuple-element.43, ...), kind=kLoop, calls=%fused_computation.74 | loop fusion | flops 786432 | bytes 792644 | tf_op jit(solution)/shard_map/convert_element_type | solution.py:139
  (36 shorter events, 0.1 us)
Async XLA Ops:
  6.5 3.0 %copy-start = (bf16[3,1536,256]{2,1,0:T(8,128)(2,1)S(1)}, bf16[3,1536,256]{2,1,0:T(8,128)(2,1)}, u32[]{:S(2)}) copy-start(bf16[3,1536,256]{2,1,0:T(8,128)(2,1)} %param.15) | copy-start | bytes 7077892
  6.5 3.0 %copy-start.1 = (bf16[2,128,1536]{2,1,0:T(8,128)(2,1)S(1)}, bf16[2,128,1536]{2,1,0:T(8,128)(2,1)}, u32[]{:S(2)}) copy-start(bf16[2,128,1536]{2,1,0:T(8,128)(2,1)} %param.12) | copy-start | bytes 2359300
  6.5 3.0 %copy-start.10 = (f32[1536]{0:T(1024)S(1)}, f32[1536]{0:T(1024)}, u32[]{:S(2)}) copy-start(f32[1536]{0:T(1024)} %param.14) | copy-start | bytes 18436
  6.5 80.2 %all-reduce.2.cloned.1.call-start = ((), (), s32[]{:S(2)}) async-start(), calls=%async_computation.1 | async-start | bytes 1572864 | tf_op jit(solution)/shard_map/psum | solution.py:113
  10.4 25.2 %copy-start.7 = (s32[2]{0:T(128)S(1)}, s32[2]{0:T(128)}, u32[]{:S(2)}) copy-start(s32[2]{0:T(128)} %param.13) | copy-start | bytes 28
  10.5 30.4 %collective-permute-start = (bf16[2,128,256]{2,1,0:T(8,128)(2,1)S(1)}, bf16[2,128,256]{2,1,0:T(8,128)(2,1)}, u32[]{:S(2)}, u32[]{:S(2)}) collective-permute-start(bf16[2,128,256]{2,1,0:T(8,128)(2,1)S(1)} %get-tuple-element.39), channel_id=1, source_target_pairs={{0,4},{4,8},{8,12},{12,0},{1,5},{5,9},{9,13},{13,1},{2,6},{6,10},{... | collective-permute-start | bytes 393224 | tf_op jit(solution)/shard_map/ppermute | solution.py:20
  13.5 29.4 %collective-permute-start.1 = (bf16[2,128,256]{2,1,0:T(8,128)(2,1)S(1)}, bf16[2,128,256]{2,1,0:T(8,128)(2,1)}, u32[]{:S(2)}, u32[]{:S(2)}) collective-permute-start(bf16[2,128,256]{2,1,0:T(8,128)(2,1)S(1)} %get-tuple-element.39), channel_id=1, source_target_pairs={{0,12},{4,0},{8,4},{12,8},{1,13},{5,1},{9,5},{13,9},{2,14},{6,2},{... | collective-permute-start | bytes 393224 | tf_op jit(solution)/shard_map/ppermute | solution.py:25
  37.3 1.4 %copy-start.2 = (f32[2,4,128,512]{3,2,1,0:T(8,128)}, f32[2,4,128,512]{3,2,1,0:T(8,128)S(1)}, u32[]{:S(2)}) copy-start(f32[2,4,128,512]{3,2,1,0:T(8,128)S(1)} %get-tuple-element.46) | copy-start | bytes 6291460
  41.9 7.0 %collective-permute-start.2 = (bf16[2,128,256]{2,1,0:T(8,128)(2,1)}, bf16[2,128,256]{2,1,0:T(8,128)(2,1)S(1)}, u32[]{:S(2)}, u32[]{:S(2)}) collective-permute-start(bf16[2,128,256]{2,1,0:T(8,128)(2,1)} %collective-permute-done), channel_id=1, source_target_pairs={{0,4},{4,8},{8,12},{12,0},{1,5},{5,9},{9,13},{13,1},{2,6},{6,10},{... | collective-permute-start | bytes 393224 | tf_op jit(solution)/shard_map/ppermute | solution.py:20
  49.7 2.4 %copy-start.4 = (bf16[256,1536]{1,0:T(8,128)(2,1)S(1)}, bf16[256,1536]{1,0:T(8,128)(2,1)}, u32[]{:S(2)}) copy-start(bf16[256,1536]{1,0:T(8,128)(2,1)} %param.16) | copy-start | bytes 2359300
  52.2 1.4 %copy-start.5 = (f32[31,384]{1,0:T(8,128)S(1)}, f32[31,384]{1,0:T(8,128)}, u32[]{:S(2)}) copy-start(f32[31,384]{1,0:T(8,128)} %param.19) | copy-start | bytes 142852
  53.5 73.0 %reduce-scatter.2.cloned.1.call-start = ((), (), s32[]{:S(2)}) async-start(), calls=%async_computation.2 | async-start | bytes 983040 | tf_op jit(solution)/shard_map/reduce_scatter | solution.py:131
  86.8 2.7 %copy-start.3 = (bf16[2,128,1536]{2,1,0:T(8,128)(2,1)S(1)}, bf16[2,128,1536]{2,1,0:T(8,128)(2,1)}, u32[]{:S(2)}) copy-start(bf16[2,128,1536]{2,1,0:T(8,128)(2,1)} %all-reduce.2.cloned.1.call-done) | copy-start | bytes 2359300
  86.8 3.1 %copy-start.8 = (bf16[2,1536,384]{2,1,0:T(8,128)(2,1)S(1)}, bf16[2,1536,384]{2,1,0:T(8,128)(2,1)}, u32[]{:S(2)}) copy-start(bf16[2,1536,384]{2,1,0:T(8,128)(2,1)} %param.18) | copy-start | bytes 7077892
  89.4 0.7 copy-start.11
  90.1 10.3 %copy-start.9 = (bf16[384,1536]{1,0:T(8,128)(2,1)S(1)}, bf16[384,1536]{1,0:T(8,128)(2,1)}, u32[]{:S(2)}) copy-start(bf16[384,1536]{1,0:T(8,128)(2,1)} %param.22) | copy-start | bytes 3538948
  90.1 10.3 %copy-start.12 = (f32[384]{0:T(512)S(1)}, f32[384]{0:T(512)}, u32[]{:S(2)}) copy-start(f32[384]{0:T(512)} %param.21) | copy-start | bytes 4612
  90.1 10.3 %copy-start.13 = (f32[384]{0:T(512)S(1)}, f32[384]{0:T(512)}, u32[]{:S(2)}) copy-start(f32[384]{0:T(512)} %param.20) | copy-start | bytes 4612
  91.2 4.9 %collective-permute-start.3 = (bf16[2,15,384]{2,1,0:T(8,128)(2,1)S(1)}, bf16[2,15,384]{2,1,0:T(8,128)(2,1)S(1)}, u32[]{:S(2)}, u32[]{:S(2)}) collective-permute-start(bf16[2,15,384]{2,1,0:T(8,128)(2,1)S(1)} %get-tuple-element.41), channel_id=1, source_target_pairs={{0,4},{4,8},{8,12},{1,5},{5,9},{9,13},{2,6},{6,10},{10,14},{3,7},{... | collective-permute-start | bytes 69128 | tf_op jit(solution)/shard_map/ppermute | solution.py:39
  94.6 5.7 %collective-permute-start.4 = (bf16[2,15,384]{2,1,0:T(8,128)(2,1)S(1)}, bf16[2,15,384]{2,1,0:T(8,128)(2,1)S(1)}, u32[]{:S(2)}, u32[]{:S(2)}) collective-permute-start(bf16[2,15,384]{2,1,0:T(8,128)(2,1)S(1)} %get-tuple-element.42), channel_id=1, source_target_pairs={{4,0},{8,4},{12,8},{5,1},{9,5},{13,9},{6,2},{10,6},{14,10},{7,3},{... | collective-permute-start | bytes 69128 | tf_op jit(solution)/shard_map/ppermute | solution.py:40
  100.4 3.7 %copy-start.6 = (s32[1536]{0:T(1024)S(1)}, s32[1536]{0:T(1024)}, u32[]{:S(2)}) copy-start(s32[1536]{0:T(1024)} %param.23) | copy-start | bytes 18436
Sparse Core Ops, SparseCore 0:
  53.6 33.1 all-reduce.1
  104.0 22.3 reduce-scatter.1
